TPU v7x, 32 devices: a whole 2x2x4 slice. The times are simulated.
32 devices in a mesh: clips: 2 (over y), tm: 4 (over x, core), rows: 4 (over z).
Axes of the slice: x: 2, y: 2, z: 4, core: 2. Of those that a mesh axis runs over, the one named last changes fastest.
Arguments:
- segment_input: bfloat16 [4, 8, 4, 32, 384], P('clips', 'tm', 'rows'), parts along dimension 0, may hold values from -6 to 6
- inner_input: bfloat16 [4, 8, 4, 32, 384], P('clips', 'tm', 'rows'), parts along dimension 0, may hold values from -6 to 6
- lengths: int32 [4, 4], P('clips', 'tm'), parts along dimension 0, may hold values from 1 to 2
- inner_gain: float32 [384], replicated, may hold values from 0.25 to 1.75
- causal_weight: bfloat16 [3, 3, 3, 384, 384], replicated, may hold values from -0.0625 to 0.0625
- causal_bias: float32 [384], replicated, may hold values from -3 to 3
- attention_gain: float32 [384], replicated, may hold values from 0.25 to 1.75
- triple_weight: bfloat16 [384, 1152], replicated, may hold values from -0.4375 to 0.4375
- triple_bias: float32 [1152], replicated, may hold values from -150 to 150
- output_weight: bfloat16 [384, 384], replicated, may hold values from -0.3125 to 0.3125
- output_bias: float32 [384], replicated, may hold values from -3 to 3
Outputs:
- encoded: bfloat16 [4, 8, 4, 32, 384], P('clips', 'tm', 'rows'), parts along dimension 0
There are 2 independent parts, one for each index of `clips`. A program takes and returns all parts, laid end to end along the dimension named above; an argument that names none is the same for every part. Nothing has to cross between parts.
Inputs may be any that keep to these rules, and one draw needn't show every extreme that they name: The valid frames of a clip in a section are that section's first lengths[b, s] frame slots.
All inputs are finite; a program needn't handle non-finite values.
Results may differ from a plain program's by a relative error of at most 0.0062.
Values may be sent and summed in bfloat16 or wider, within the bound.
No kernel may reach another device: no remote copies, remote signals or barrier semaphores. Data moves between devices by JAX's collectives and lax.ppermute only.
A program may use at most 128 MiB of HBM per device.

v0:
```python
import math
import jax
import jax.numpy as jnp
from jax import lax
from jax.sharding import PartitionSpec as P

EPSILON = 1e-06


def prefix(part, axis, combine, identity):
    place = lax.axis_index(axis)
    gathered = jax.tree.map(lambda a: lax.all_gather(a, axis), part)
    state = jax.tree.map(lambda a, e: jnp.zeros_like(a) + jnp.asarray(e, a.dtype), part, identity)

    def one(step, state):
        return combine(
            state, jax.tree.map(lambda a: lax.dynamic_index_in_dim(a, step, 0, False), gathered)
        )

    return lax.fori_loop(0, place, one, state)


def as_sent(x):

    def short(part):
        return part.astype(jnp.bfloat16) if part.dtype == jnp.float32 else part

    return jax.tree.map(short, x)


def with_halo(cells, sides, width):
    for axis, dim in sides:
        count = lax.axis_size(axis)
        ends = count - 1
        head = lax.slice_in_dim(cells, 0, width, axis=dim)
        tail = lax.slice_in_dim(cells, cells.shape[dim] - width, cells.shape[dim], axis=dim)
        cells = jnp.concatenate(
            [
                lax.ppermute(tail, axis, [(i, (i + 1) % count) for i in range(ends)]),
                cells,
                lax.ppermute(head, axis, [((i + 1) % count, i) for i in range(ends)]),
            ],
            axis=dim,
        )
    return cells


def normalize(field, gain):
    widened = field.astype(jnp.float32)
    return widened * lax.rsqrt(jnp.mean(widened * widened, axis=-1, keepdims=True) + EPSILON) * gain


def last_two(extended, counts):
    slot_total = extended.shape[1]
    chosen = []
    for position in range(2):
        target = counts + position
        picked = jnp.zeros_like(extended[:, 0])
        for slot_index in range(slot_total):
            matches = (target == slot_index)[:, None, None, None]
            picked = jnp.where(matches, extended[:, slot_index], picked)
        chosen.append(picked)
    return jnp.stack(chosen, axis=1)


def summarize(activated, counts):
    blanks = jnp.zeros((activated.shape[0], 2) + activated.shape[2:], activated.dtype)
    summary = last_two(jnp.concatenate([blanks, activated], axis=1), counts)
    return (summary, jnp.minimum(counts, 2).astype(jnp.bfloat16))


def join_later(earlier, later):
    early_frames, early_count = earlier
    late_frames, late_count = later
    complete = (late_count > 1.5)[:, None, None, None, None]
    single = (late_count > 0.5)[:, None, None, None, None]
    shifted = jnp.concatenate([early_frames[:, 1:], late_frames[:, 1:]], axis=1)
    frames = jnp.where(complete, late_frames, jnp.where(single, shifted, early_frames))
    total_count = jnp.minimum(early_count + late_count, 2.0).astype(early_count.dtype)
    return (frames, total_count)


def incoming_cache(summary, counts):
    starting = (jnp.zeros_like(summary), jnp.zeros_like(counts))
    combined = prefix((summary, counts), "tm", join_later, starting)
    return combined[0]


def convolve(padded, causal_weight, causal_bias):
    clip_count, slot_total, rows_padded, column_count, channels = padded.shape
    frame_count = slot_total - 2
    row_count = rows_padded - 2
    widened = jnp.pad(padded, ((0, 0), (0, 0), (0, 0), (1, 1), (0, 0)))
    summed = jnp.zeros((clip_count * frame_count * row_count * column_count, channels), jnp.float32)
    for delta_time in range(3):
        for delta_row in range(3):
            window = widened[
                :, delta_time : delta_time + frame_count, delta_row : delta_row + row_count
            ]
            columns = jnp.concatenate(
                [window[:, :, :, delta_col : delta_col + column_count] for delta_col in range(3)],
                axis=-1,
            )
            kernel = causal_weight[delta_time, delta_row].reshape(3 * channels, channels)
            summed = summed + jnp.dot(
                columns.reshape(-1, 3 * channels), kernel, preferred_element_type=jnp.float32
            )
    return summed.reshape(clip_count, frame_count, row_count, column_count, channels) + causal_bias


def attend(normed, triple_weight, triple_bias, output_weight, output_bias):
    frame_count, places, channels = normed.shape
    packed = (
        jnp.dot(normed.reshape(-1, channels), triple_weight, preferred_element_type=jnp.float32)
        + triple_bias
    )
    packed = packed.reshape(frame_count, places, 3 * channels)
    queries = packed[:, :, :channels]
    key_vectors = packed[:, :, channels : 2 * channels]
    values = packed[:, :, 2 * channels :].astype(jnp.bfloat16)
    scores = jnp.einsum(
        "nqc,nkc->nqk", queries, key_vectors, precision=lax.Precision.HIGHEST
    ) / math.sqrt(channels)
    row_max = jnp.max(scores, axis=-1, keepdims=True)
    exponent = jnp.exp(scores - row_max)
    weights = (exponent / jnp.sum(exponent, axis=-1, keepdims=True)).astype(jnp.bfloat16)
    attended = jnp.einsum(
        "nqk,nkc->nqc", weights, values, preferred_element_type=jnp.float32
    ).astype(jnp.bfloat16)
    projected = (
        jnp.dot(attended.reshape(-1, channels), output_weight, preferred_element_type=jnp.float32)
        + output_bias
    )
    return projected.reshape(frame_count, places, channels).astype(jnp.bfloat16)


def body(
    segment_input,
    inner_input,
    lengths,
    inner_gain,
    causal_weight,
    causal_bias,
    attention_gain,
    triple_weight,
    triple_bias,
    output_weight,
    output_bias,
):
    clip_count, frame_count, row_count, column_count, channels = segment_input.shape
    activated = jax.nn.silu(normalize(inner_input, inner_gain)).astype(jnp.bfloat16)
    counts = lengths[:, 0]
    live_mask = (jnp.arange(frame_count, dtype=jnp.int32)[None, :] < counts[:, None]).astype(
        jnp.float32
    )
    carried = incoming_cache(*summarize(activated, counts))
    extended = jnp.concatenate([carried, activated], axis=1)
    padded = with_halo(as_sent(extended), (("rows", 2),), 1).astype(extended.dtype)
    convolved = convolve(padded, causal_weight, causal_bias)
    residual = (segment_input.astype(jnp.float32) + convolved).astype(jnp.bfloat16)
    residual = lax.optimization_barrier(residual)
    normed = normalize(residual, attention_gain).astype(jnp.bfloat16)
    row_devices = lax.axis_size("rows")
    per_device = clip_count * frame_count // row_devices
    grouped = normed.reshape(row_devices, per_device, row_count, column_count, channels)
    portion = lax.all_to_all(grouped, "rows", split_axis=0, concat_axis=2, tiled=True)
    owned = portion.shape[1]
    height = portion.shape[2]
    flat = portion.reshape(owned, height * column_count, channels)
    result = attend(flat, triple_weight, triple_bias, output_weight, output_bias)
    result = result.reshape(1, owned, height, column_count, channels)
    projected = lax.all_to_all(result, "rows", split_axis=2, concat_axis=0, tiled=True)
    projected = projected.reshape(clip_count, frame_count, row_count, column_count, channels)
    projected = lax.optimization_barrier(projected)
    summed = residual.astype(jnp.float32) + projected.astype(jnp.float32)
    return (summed * live_mask[:, :, None, None, None]).astype(jnp.bfloat16)


def activate(field, gain):
    return jax.nn.silu(normalize(field, gain)).astype(jnp.bfloat16)


def gathered_body(
    segment_input,
    inner_input,
    lengths,
    inner_gain,
    causal_weight,
    causal_bias,
    attention_gain,
    triple_weight,
    triple_bias,
    output_weight,
    output_bias,
):
    clip_count, frame_count, row_count, column_count, channels = segment_input.shape
    sections = lax.axis_size("tm")
    inner_all = lax.all_gather(inner_input, "rows", axis=2, tiled=True)
    segment_all = lax.all_gather(segment_input, "rows", axis=2, tiled=True)
    counts = lengths[:, 0]
    wide = (counts > 1)[:, None, None, None]
    last_raw = jnp.where(wide, inner_all[:, frame_count - 1], inner_all[:, 0])
    prev_raw = lax.ppermute(inner_all, "tm", [(i, i + 1) for i in range(sections - 1)])
    prev_counts = lax.ppermute(counts, "tm", [(i, i + 1) for i in range(sections - 1)])
    before_raw = lax.ppermute(last_raw, "tm", [(i, i + 2) for i in range(sections - 2)])
    own = activate(inner_all, inner_gain)
    prev = activate(prev_raw, inner_gain)
    before = activate(before_raw, inner_gain)
    prev_wide = (prev_counts > 1)[:, None, None, None]
    carried = jnp.stack(
        [
            jnp.where(prev_wide, prev[:, frame_count - 2], before),
            jnp.where(prev_wide, prev[:, frame_count - 1], prev[:, 0]),
        ],
        axis=1,
    )
    extended = jnp.concatenate([carried, own], axis=1)
    padded = jnp.pad(extended, ((0, 0), (0, 0), (1, 1), (0, 0), (0, 0)))
    convolved = convolve(padded, causal_weight, causal_bias)
    residual = (segment_all.astype(jnp.float32) + convolved).astype(jnp.bfloat16)
    normed = normalize(residual, attention_gain).astype(jnp.bfloat16)
    height = normed.shape[2]
    frames = clip_count * frame_count
    places = height * column_count
    flat = normed.reshape(frames * places, channels)
    packed = (
        jnp.dot(flat, triple_weight[:, channels:], preferred_element_type=jnp.float32)
        + triple_bias[channels:]
    ).reshape(frames, places, 2 * channels)
    key_vectors = packed[:, :, :channels]
    values = packed[:, :, channels:].astype(jnp.bfloat16)
    start = lax.axis_index("rows") * row_count
    mine = lax.dynamic_slice_in_dim(normed, start, row_count, axis=2)
    queries = (
        jnp.dot(
            mine.reshape(-1, channels),
            triple_weight[:, :channels],
            preferred_element_type=jnp.float32,
        )
        + triple_bias[:channels]
    ).reshape(frames, row_count * column_count, channels)
    scores = jnp.einsum(
        "nqc,nkc->nqk", queries, key_vectors, precision=lax.Precision.HIGHEST
    ) / math.sqrt(channels)
    row_max = jnp.max(scores, axis=-1, keepdims=True)
    exponent = jnp.exp(scores - row_max)
    weights = (exponent / jnp.sum(exponent, axis=-1, keepdims=True)).astype(jnp.bfloat16)
    attended = jnp.einsum(
        "nqk,nkc->nqc", weights, values, preferred_element_type=jnp.float32
    ).astype(jnp.bfloat16)
    projected = (
        jnp.dot(attended.reshape(-1, channels), output_weight, preferred_element_type=jnp.float32)
        + output_bias
    ).astype(jnp.bfloat16)
    projected = projected.reshape(clip_count, frame_count, row_count, column_count, channels)
    residual_mine = lax.dynamic_slice_in_dim(residual, start, row_count, axis=2)
    live_mask = (jnp.arange(frame_count, dtype=jnp.int32)[None, :] < counts[:, None]).astype(
        jnp.float32
    )
    summed = residual_mine.astype(jnp.float32) + projected.astype(jnp.float32)
    return (summed * live_mask[:, :, None, None, None]).astype(jnp.bfloat16)


GATHER_LIMIT = 1 << 22


def chosen_body(segment_input, inner_input, *rest):
    gathered = inner_input.size * inner_input.dtype.itemsize * lax.axis_size("rows")
    if gathered <= GATHER_LIMIT:
        return gathered_body(segment_input, inner_input, *rest)
    return body(segment_input, inner_input, *rest)


def solution(mesh):
    placed = (
        P("clips", "tm", "rows", None, None),
        P("clips", "tm", "rows", None, None),
        P("clips", "tm"),
        P(),
        P(),
        P(),
        P(),
        P(),
        P(),
        P(),
        P(),
    )
    return jax.shard_map(
        chosen_body,
        mesh=mesh,
        in_specs=placed,
        out_specs=P("clips", "tm", "rows", None, None),
        check_vma=False,
    )
```

profile of v0, /device:TPU:0, one launch (start us, length us, event | category | flops | bytes accessed | tf_op | source)
XLA Modules:
  0.0 70.2 jit_solution(4416258537205051209)
XLA Ops:
  0.0 16.6 %all_gather.7 = bf16[2,2,4,32,384]{4,3,2,1,0:T(8,128)(2,1)S(1)} all-gather(bf16[2,2,1,32,384]{4,3,2,1,0:T(8,128)(2,1)} %param.12), channel_id=1, replica_groups=mesh['clips'=2,'tm'=4,'rows'=4] {'rows'}, dimensions={2}, use_global_device_ids=true | all-gather | bytes 491520 | tf_op jit(solution)/shard_map/all_gather | solution.py:198
  16.6 0.8 %copy.33 = bf16[2,2,4,32,384]{4,3,2,0,1:T(8,128)(2,1)} copy(bf16[2,2,4,32,384]{4,3,2,1,0:T(8,128)(2,1)S(1)} %all_gather.7) | data formatting | bytes 786432 | tf_op jit(solution)/shard_map/all_gather | solution.py:198
  17.4 1.3 %collective-permute-start.1 = (bf16[2,2,4,32,384]{4,3,2,0,1:T(8,128)(2,1)}, bf16[2,2,4,32,384]{4,3,2,0,1:T(8,128)(2,1)S(1)}, u32[]{:S(2)}, u32[]{:S(2)}) collective-permute-start(bf16[2,2,4,32,384]{4,3,2,0,1:T(8,128)(2,1)} %copy.33), channel_id=1, source_target_pairs={{0,4},{4,8},{8,12},{1,5},{5,9},{9,13},{2,6},{6,10},{10,14},{3,7},{... | collective-permute-start | bytes 1179656 | tf_op jit(solution)/shard_map/ppermute | solution.py:203
  19.4 0.8 %fusion.42 = bf16[2,4,32,384]{3,2,1,0:T(8,128)(2,1)} fusion(pred[2]{0:T(512)(128)(4,1)S(1)} %broadcast_compare_fusion, bf16[2,2,4,32,384]{4,3,2,1,0:T(8,128)(2,1)S(1)} %all_gather.7), kind=kLoop, calls=%fused_computation.98 | loop fusion | flops 98304 | bytes 589826 | tf_op jit(solution)/shard_map/jit(_where)/select_n | solution.py:202
  20.2 4.0 %collective-permute-start.2 = (bf16[2,4,32,384]{3,2,1,0:T(8,128)(2,1)}, bf16[2,4,32,384]{3,2,1,0:T(8,128)(2,1)S(1)}, u32[]{:S(2)}, u32[]{:S(2)}) collective-permute-start(bf16[2,4,32,384]{3,2,1,0:T(8,128)(2,1)} %fusion.42), channel_id=1, source_target_pairs={{0,8},{4,12},{1,9},{5,13},{2,10},{6,14},{3,11},{7,15},{16,24},{20,... | collective-permute-start | bytes 589832 | tf_op jit(solution)/shard_map/ppermute | solution.py:205
  24.2 1.4 %collective-permute-start = (s32[2]{0:T(128)S(1)}, s32[2]{0:T(128)S(1)}, u32[]{:S(2)}, u32[]{:S(2)}) collective-permute-start(s32[2]{0:T(128)S(1)} %bitcast.102), channel_id=1, source_target_pairs={{0,4},{4,8},{8,12},{1,5},{5,9},{9,13},{2,6},{6,10},{10,14},{3,7},{... | collective-permute-start | bytes 32 | tf_op jit(solution)/shard_map/ppermute | solution.py:204
  25.9 5.4 %fusion.52 = (bf16[1,1,3,384,384]{4,3,2,1,0:T(8,128)(2,1)S(1)}, bf16[1,1,3,384,384]{4,3,2,1,0:T(8,128)(2,1)}, bf16[1,1,3,384,384]{4,3,2,1,0:T(8,128)(2,1)}, bf16...) fusion(bf16[3,3,3,384,384]{4,3,2,1,0:T(8,128)(2,1)} %param.15), kind=kLoop, calls=%fused_computation.119 | loop fusion | bytes 15925248 | tf_op jit(solution)/shard_map/slice | solution.py:104
  31.3 16.0 %all_gather.6 = bf16[2,2,4,32,384]{4,3,2,1,0:T(8,128)(2,1)} all-gather(bf16[2,2,1,32,384]{4,3,2,1,0:T(8,128)(2,1)S(1)} %copy-done.10), channel_id=1, replica_groups=mesh['clips'=2,'tm'=4,'rows'=4] {'rows'}, dimensions={2}, use_global_device_ids=true | all-gather | bytes 491520 | tf_op jit(solution)/shard_map/all_gather | solution.py:199
  48.9 3.5 %pad_slice_fusion.1 = (bf16[2,2,4,32,384]{4,3,2,1,0:T(8,128)(2,1)S(1)}, bf16[2,2,4,32,384]{4,3,2,1,0:T(8,128)(2,1)S(1)}, bf16[2,2,4,32,384]{4,3,2,1,0:T(8,128)(2...) fusion(bf16[2,4,6,32,384]{4,3,2,1,0:T(8,128)(2,1)S(1)} %fusion.6), kind=kLoop, calls=%fused_computation.37 | loop fusion | bytes 9437184 | tf_op jit(solution)/shard_map/slice | solution.py:101
  53.0 0.9 %copy-done.9 = bf16[1,1,3,384,384]{4,3,2,1,0:T(8,128)(2,1)S(1)} copy-done((bf16[1,1,3,384,384]{4,3,2,1,0:T(8,128)(2,1)S(1)}, bf16[1,1,3,384,384]{4,3,2,1,0:T(8,128)(2,1)}, u32[]{:S(2)}) %copy-start.9) | copy-done | bytes 884760
  53.9 0.8 %fusion.55 = f32[512,384]{1,0:T(8,128)S(1)} fusion(bf16[512,1152]{1,0:T(8,128)(2,1)S(1)} %bitcast.96, bf16[1152,384]{1,0:T(8,128)(2,1)S(1)} %bitcast.97), kind=kOutput, calls=%fused_computation.122 | convolution fusion | flops 452984832 | bytes 2850816 | tf_op jit(solution)/shard_map/dot_general | solution.py:105
  55.1 0.7 %copy-done.6 = bf16[1,1,3,384,384]{4,3,2,1,0:T(8,128)(2,1)S(1)} copy-done((bf16[1,1,3,384,384]{4,3,2,1,0:T(8,128)(2,1)S(1)}, bf16[1,1,3,384,384]{4,3,2,1,0:T(8,128)(2,1)}, u32[]{:S(2)}) %copy-start.6) | copy-done | bytes 884760
  55.8 0.8 %convolution_add_fusion.8 = f32[512,384]{1,0:T(8,128)S(1)} fusion(f32[512,384]{1,0:T(8,128)S(1)} %fusion.55, bf16[512,1152]{1,0:T(8,128)(2,1)S(1)} %bitcast.80, bf16[1152,384]{1,0:T(8,128)(2,1)S(1)} %bitcast.93), kind=kOutput, calls=%fused_computation.15 | convolution fusion | flops 453181440 | bytes 3637248 | tf_op jit(solution)/shard_map/dot_general | solution.py:105
  57.0 0.8 %convolution_add_fusion.7 = f32[512,384]{1,0:T(8,128)S(1)} fusion(f32[512,384]{1,0:T(8,128)S(1)} %convolution_add_fusion.8, bf16[512,1152]{1,0:T(8,128)(2,1)S(1)} %bitcast.81, bf16[1152,384]{1,0:T(8,128)(2,1)S(1)} %bitcast.92), kind=kOutput, calls=%fused_computation.14 | convolution fusion | flops 453181440 | bytes 3637248 | tf_op jit(solution)/shard_map/dot_general | solution.py:105
  58.1 0.9 %copy-done.4 = bf16[1,1,3,384,384]{4,3,2,1,0:T(8,128)(2,1)S(1)} copy-done((bf16[1,1,3,384,384]{4,3,2,1,0:T(8,128)(2,1)S(1)}, bf16[1,1,3,384,384]{4,3,2,1,0:T(8,128)(2,1)}, u32[]{:S(2)}) %copy-start.4) | copy-done | bytes 884760
  59.0 0.8 %convolution_add_fusion.6 = f32[512,384]{1,0:T(8,128)S(1)} fusion(f32[512,384]{1,0:T(8,128)S(1)} %convolution_add_fusion.7, bf16[512,1152]{1,0:T(8,128)(2,1)S(1)} %bitcast.84, bf16[1152,384]{1,0:T(8,128)(2,1)S(1)} %bitcast.91), kind=kOutput, calls=%fused_computation.13 | convolution fusion | flops 453181440 | bytes 3637248 | tf_op jit(solution)/shard_map/dot_general | solution.py:105
  60.1 0.8 %convolution_add_fusion.5 = f32[512,384]{1,0:T(8,128)S(1)} fusion(f32[512,384]{1,0:T(8,128)S(1)} %convolution_add_fusion.6, bf16[512,1152]{1,0:T(8,128)(2,1)S(1)} %bitcast.79, bf16[1152,384]{1,0:T(8,128)(2,1)S(1)} %bitcast.90), kind=kOutput, calls=%fused_computation.12 | convolution fusion | flops 453181440 | bytes 3637248 | tf_op jit(solution)/shard_map/dot_general | solution.py:105
  61.3 0.8 %convolution_add_fusion.4 = f32[512,384]{1,0:T(8,128)S(1)} fusion(f32[512,384]{1,0:T(8,128)S(1)} %convolution_add_fusion.5, bf16[512,1152]{1,0:T(8,128)(2,1)S(1)} %bitcast.83, bf16[1152,384]{1,0:T(8,128)(2,1)S(1)} %bitcast.89), kind=kOutput, calls=%fused_computation.11 | convolution fusion | flops 453181440 | bytes 3637248 | tf_op jit(solution)/shard_map/dot_general | solution.py:105
  62.4 0.9 %copy-done.1 = bf16[1,1,3,384,384]{4,3,2,1,0:T(8,128)(2,1)S(1)} copy-done((bf16[1,1,3,384,384]{4,3,2,1,0:T(8,128)(2,1)S(1)}, bf16[1,1,3,384,384]{4,3,2,1,0:T(8,128)(2,1)}, u32[]{:S(2)}) %copy-start.1) | copy-done | bytes 884760
  63.3 0.8 %convolution_add_fusion.3 = f32[512,384]{1,0:T(8,128)S(1)} fusion(f32[512,384]{1,0:T(8,128)S(1)} %convolution_add_fusion.4, bf16[512,1152]{1,0:T(8,128)(2,1)S(1)} %bitcast.85, bf16[1152,384]{1,0:T(8,128)(2,1)S(1)} %bitcast.88), kind=kOutput, calls=%fused_computation.10 | convolution fusion | flops 453181440 | bytes 3637248 | tf_op jit(solution)/shard_map/dot_general | solution.py:105
  64.1 0.8 %convolution_add_fusion.2 = f32[512,384]{1,0:T(8,128)S(1)} fusion(f32[512,384]{1,0:T(8,128)S(1)} %convolution_add_fusion.3, bf16[512,1152]{1,0:T(8,128)(2,1)S(1)} %bitcast.78, bf16[1152,384]{1,0:T(8,128)(2,1)S(1)} %bitcast.87), kind=kOutput, calls=%fused_computation.9 | convolution fusion | flops 453181440 | bytes 3637248 | tf_op jit(solution)/shard_map/dot_general | solution.py:105
  64.9 0.8 %convolution_add_fusion.1 = f32[512,384]{1,0:T(8,128)S(1)} fusion(f32[512,384]{1,0:T(8,128)S(1)} %convolution_add_fusion.2, bf16[512,1152]{1,0:T(8,128)(2,1)S(1)} %bitcast.82, bf16[1152,384]{1,0:T(8,128)(2,1)S(1)} %bitcast.86), kind=kOutput, calls=%fused_computation.8 | convolution fusion | flops 453181440 | bytes 3637248 | tf_op jit(solution)/shard_map/dot_general | solution.py:105
  67.7 1.0 %convolution_multiply_fusion = f32[4,32,128]{2,1,0:T(8,128)S(1)} fusion(f32[4,32,384]{2,1,0:T(8,128)S(1)} %bitcast.98, f32[4,128,768]{2,1,0:T(8,128)S(1)} %bitcast.76), kind=kOutput, calls=%fused_computation.35 | convolution fusion | flops 75513856 | bytes 1048576 | tf_op jit(solution)/shard_map/nqc,nkc->nqk/dot_general | solution.py:242
  69.4 0.7 %fusion.44 = bf16[2,2,1,32,384]{4,3,2,1,0:T(8,128)(2,1)} fusion(bf16[2,2,1,32,384]{4,3,2,1,0:T(8,128)(2,1)S(1)} %bitcast.101, f32[2,2]{1,0:T(2,128)S(1)} %compare_convert_fusion, bf16[2,2,4,32,384]{4,3,2,1,0:T(8,128)(2,1)S(1)} %get-tuple-element.6, s32[]{:T(128)S(6)} %select_n.18), kind=kLoop, calls=%fused_computation.102 | loop fusion | flops 245760 | bytes 294932 | tf_op jit(solution)/shard_map/convert_element_type | solution.py:261
  (63 shorter events, 7.6 us)
Async XLA Ops:
  0.0 69.2 %copy-start = (bf16[384,384]{1,0:T(8,128)(2,1)S(1)}, bf16[384,384]{1,0:T(8,128)(2,1)}, u32[]{:S(2)}) copy-start(bf16[384,384]{1,0:T(8,128)(2,1)} %param.20) | copy-start | bytes 884740
  0.0 24.2 %copy-start.16 = (s32[2,1]{0,1:T(1,128)S(1)}, s32[2,1]{0,1:T(1,128)}, u32[]{:S(2)}) copy-start(s32[2,1]{0,1:T(1,128)} %param.13) | copy-start | bytes 28
  0.0 25.7 %copy-start.12 = (f32[1152]{0:T(1024)S(1)}, f32[1152]{0:T(1024)}, u32[]{:S(2)}) copy-start(f32[1152]{0:T(1024)} %param.19) | copy-start | bytes 13828
  17.4 30.5 %collective-permute-start.1 = (bf16[2,2,4,32,384]{4,3,2,0,1:T(8,128)(2,1)}, bf16[2,2,4,32,384]{4,3,2,0,1:T(8,128)(2,1)S(1)}, u32[]{:S(2)}, u32[]{:S(2)}) collective-permute-start(bf16[2,2,4,32,384]{4,3,2,0,1:T(8,128)(2,1)} %copy.33), channel_id=1, source_target_pairs={{0,4},{4,8},{8,12},{1,5},{5,9},{9,13},{2,6},{6,10},{10,14},{3,7},{... | collective-permute-start | bytes 1179656 | tf_op jit(solution)/shard_map/ppermute | solution.py:203
  20.2 27.6 %collective-permute-start.2 = (bf16[2,4,32,384]{3,2,1,0:T(8,128)(2,1)}, bf16[2,4,32,384]{3,2,1,0:T(8,128)(2,1)S(1)}, u32[]{:S(2)}, u32[]{:S(2)}) collective-permute-start(bf16[2,4,32,384]{3,2,1,0:T(8,128)(2,1)} %fusion.42), channel_id=1, source_target_pairs={{0,8},{4,12},{1,9},{5,13},{2,10},{6,14},{3,11},{7,15},{16,24},{20,... | collective-permute-start | bytes 589832 | tf_op jit(solution)/shard_map/ppermute | solution.py:205
  24.2 23.5 %collective-permute-start = (s32[2]{0:T(128)S(1)}, s32[2]{0:T(128)S(1)}, u32[]{:S(2)}, u32[]{:S(2)}) collective-permute-start(s32[2]{0:T(128)S(1)} %bitcast.102), channel_id=1, source_target_pairs={{0,4},{4,8},{8,12},{1,5},{5,9},{9,13},{2,6},{6,10},{10,14},{3,7},{... | collective-permute-start | bytes 32 | tf_op jit(solution)/shard_map/ppermute | solution.py:204
  25.9 5.5 %copy-start.10 = (bf16[2,2,1,32,384]{4,3,2,1,0:T(8,128)(2,1)S(1)}, bf16[2,2,1,32,384]{4,3,2,1,0:T(8,128)(2,1)}, u32[]{:S(2)}) copy-start(bf16[2,2,1,32,384]{4,3,2,1,0:T(8,128)(2,1)} %param.11) | copy-start | bytes 294916
  25.9 21.5 %copy-start.11 = (f32[384]{0:T(512)S(1)}, f32[384]{0:T(512)}, u32[]{:S(2)}) copy-start(f32[384]{0:T(512)} %param.14) | copy-start | bytes 4612
  52.7 1.2 %copy-start.9 = (bf16[1,1,3,384,384]{4,3,2,1,0:T(8,128)(2,1)S(1)}, bf16[1,1,3,384,384]{4,3,2,1,0:T(8,128)(2,1)}, u32[]{:S(2)}) copy-start(bf16[1,1,3,384,384]{4,3,2,1,0:T(8,128)(2,1)} %get-tuple-element.14) | copy-start | bytes 2654212
  54.7 1.2 %copy-start.6 = (bf16[1,1,3,384,384]{4,3,2,1,0:T(8,128)(2,1)S(1)}, bf16[1,1,3,384,384]{4,3,2,1,0:T(8,128)(2,1)}, u32[]{:S(2)}) copy-start(bf16[1,1,3,384,384]{4,3,2,1,0:T(8,128)(2,1)} %get-tuple-element.13) | copy-start | bytes 2654212
  55.8 1.2 %copy-start.5 = (bf16[1,1,3,384,384]{4,3,2,1,0:T(8,128)(2,1)S(1)}, bf16[1,1,3,384,384]{4,3,2,1,0:T(8,128)(2,1)}, u32[]{:S(2)}) copy-start(bf16[1,1,3,384,384]{4,3,2,1,0:T(8,128)(2,1)} %get-tuple-element.12) | copy-start | bytes 2654212
  57.8 1.2 %copy-start.4 = (bf16[1,1,3,384,384]{4,3,2,1,0:T(8,128)(2,1)S(1)}, bf16[1,1,3,384,384]{4,3,2,1,0:T(8,128)(2,1)}, u32[]{:S(2)}) copy-start(bf16[1,1,3,384,384]{4,3,2,1,0:T(8,128)(2,1)} %get-tuple-element.11) | copy-start | bytes 2654212
  59.0 1.2 %copy-start.3 = (bf16[1,1,3,384,384]{4,3,2,1,0:T(8,128)(2,1)S(1)}, bf16[1,1,3,384,384]{4,3,2,1,0:T(8,128)(2,1)}, u32[]{:S(2)}) copy-start(bf16[1,1,3,384,384]{4,3,2,1,0:T(8,128)(2,1)} %get-tuple-element.10) | copy-start | bytes 2654212
  60.1 1.2 %copy-start.2 = (bf16[1,1,3,384,384]{4,3,2,1,0:T(8,128)(2,1)S(1)}, bf16[1,1,3,384,384]{4,3,2,1,0:T(8,128)(2,1)}, u32[]{:S(2)}) copy-start(bf16[1,1,3,384,384]{4,3,2,1,0:T(8,128)(2,1)} %get-tuple-element.9) | copy-start | bytes 2654212
  62.1 1.2 %copy-start.1 = (bf16[1,1,3,384,384]{4,3,2,1,0:T(8,128)(2,1)S(1)}, bf16[1,1,3,384,384]{4,3,2,1,0:T(8,128)(2,1)}, u32[]{:S(2)}) copy-start(bf16[1,1,3,384,384]{4,3,2,1,0:T(8,128)(2,1)} %get-tuple-element.8) | copy-start | bytes 2654212
  64.9 1.0 %copy-start.7 = (bf16[2,2,4,32,384]{4,3,2,1,0:T(8,128)(2,1)S(1)}, bf16[2,2,4,32,384]{4,3,2,1,0:T(8,128)(2,1)}, u32[]{:S(2)}) copy-start(bf16[2,2,4,32,384]{4,3,2,1,0:T(8,128)(2,1)} %all_gather.6) | copy-start | bytes 1179652
  64.9 1.0 %copy-start.13 = (f32[384]{0:T(512)S(1)}, f32[384]{0:T(512)}, u32[]{:S(2)}) copy-start(f32[384]{0:T(512)} %param.16) | copy-start | bytes 4612
  65.7 0.7 %copy-start.14 = (f32[384]{0:T(512)S(1)}, f32[384]{0:T(512)}, u32[]{:S(2)}) copy-start(f32[384]{0:T(512)} %param.17) | copy-start | bytes 4612
  65.7 1.2 %copy-start.8 = (bf16[384,1152]{1,0:T(8,128)(2,1)S(1)}, bf16[384,1152]{1,0:T(8,128)(2,1)}, u32[]{:S(2)}) copy-start(bf16[384,1152]{1,0:T(8,128)(2,1)} %param.18) | copy-start | bytes 2654212
  66.6 0.9 %slice-start = ((f32[1152]{0:T(1024)}), f32[384]{0:T(512)S(1)}, s32[]{:S(2)}) async-start(f32[1152]{0:T(1024)} %param.19), calls=%async_computation | async-start | bytes 4096 | tf_op jit(solution)/shard_map/slice | solution.py:240
  67.5 1.7 %copy-start.15 = (f32[384]{0:T(512)S(1)}, f32[384]{0:T(512)}, u32[]{:S(2)}) copy-start(f32[384]{0:T(512)} %param.21) | copy-start | bytes 4612
where the time goes:
time: 70.7 us; the launch traced here: 70.2 us
  blocking collectives  32.6 us (46%)
  local copies, waits for them, and re-layouts  15.4 us (22%)
  matrix products  9.39 us (13%)
  starting transfers between devices  6.7 us (9%)
  other arithmetic  5.64 us (8%)
    all_gather x1, blocking collectives, gathered_body(): inner_all = lax.all_gather(inner_input, 'rows', axis=2, tiled=True)  16.6 us
    all_gather x1, blocking collectives, gathered_body(): segment_all = lax.all_gather(segment_input, 'rows', axis=2, tiled=True)  16 us
    dot_general x9, matrix products, convolve(): jnp.dot(columns.reshape(-1, 3 * channels), kernel, preferred_element_type...  7.15 us
    slice x1, local copies, waits for them, and re-layouts, convolve(): causal_weight[delta_time, delta_row].reshape(3 * channels, channels)  5.45 us
    unnamed x34, local copies, waits for them, and re-layouts  5.33 us
    ppermute x1, starting transfers between devices, gathered_body(): lax.ppermute(last_raw, 'tm', [(i, i + 2) for i in range(sections - 2)])  4 us
    slice x2, local copies, waits for them, and re-layouts, convolve(): window[:, :, :, delta_col:delta_col + column_count]  3.81 us
  transfers between devices with their start and end apart: 3, of which 0 were waited for; matrix products, arithmetic and copies ran while one was open for 11% of the time, Pallas kernels for 0%

commit v1 on v0

--- a/solution.py
+++ b/solution.py
@@ -3,8 +3,18 @@
 import jax.numpy as jnp
 from jax import lax
 from jax.sharding import PartitionSpec as P
+from jax.lax import axis_index, axis_size, ppermute
 
 EPSILON = 1e-06
+
+
+def quarters_compute(a0, out_dim):
+    a0 = jnp.moveaxis(a0, 0, out_dim)
+    mixed_arr = a0.shape
+    raw_out = a0.reshape(
+        *mixed_arr[:out_dim], mixed_arr[out_dim] * mixed_arr[out_dim + 1], *mixed_arr[out_dim + 2 :]
+    )
+    return raw_out
 
 
 def prefix(part, axis, combine, identity):
@@ -196,7 +206,20 @@
     clip_count, frame_count, row_count, column_count, channels = segment_input.shape
     sections = lax.axis_size("tm")
     inner_all = lax.all_gather(inner_input, "rows", axis=2, tiled=True)
-    segment_all = lax.all_gather(segment_input, "rows", axis=2, tiled=True)
+
+    def series_fix(slab_in, device_axis, d_out):
+        dev_count = axis_size(device_axis)
+        rack = [(pp, (pp + 1) % dev_count) for pp in range(dev_count)]
+        inbox = [slab_in]
+        while len(inbox) < dev_count:
+            inbox.append(ppermute(inbox[-1], axis_name=device_axis, perm=rack))
+        inter = axis_index(device_axis)
+        response = jnp.stack(inbox, axis=0)
+        inbox = response[(inter - jnp.arange(dev_count)) % dev_count]
+        extra = quarters_compute(inbox, d_out)
+        return extra
+
+    segment_all = series_fix(segment_input, "rows", 2)
     counts = lengths[:, 0]
     wide = (counts > 1)[:, None, None, None]
     last_raw = jnp.where(wide, inner_all[:, frame_count - 1], inner_all[:, 0])

time: 70.7 us -> 76.9 us (1.088)
  blocking collectives: 32.6 us -> 16.6 us
  waiting for transfers between devices: 0.01 us -> 12.9 us
  other arithmetic: 5.64 us -> 10.2 us
  starting transfers between devices: 6.7 us -> 9.36 us
  local copies, waits for them, and re-layouts: 15.4 us -> 16.6 us
    all_gather x1 -> x0, blocking collectives: 16 us -> none  [gathered_body(): segment_all = lax.all_gather(segment_input, 'rows', axis=2, tiled=True)]
    ppermute x0 -> x3, waiting for transfers between devices: none -> 12.9 us  [series_fix(): inbox.append(ppermute(inbox[-1], axis_name=device_axis, perm=rack))]
    ppermute x0 -> x3, starting transfers between devices: none -> 2.18 us  [series_fix(): inbox.append(ppermute(inbox[-1], axis_name=device_axis, perm=rack))]
    gather x0 -> x1, local copies, waits for them, and re-layouts: none -> 1.75 us  [series_fix(): inbox = response[(inter - jnp.arange(dev_count)) % dev_count]]
    another operation x0 -> x1, other arithmetic: none -> 1.71 us  [series_fix(): response = jnp.stack(inbox, axis=0)]
    unnamed x34, local copies, waits for them, and re-layouts: 5.33 us -> 4.08 us
    convert_element_type x1, other arithmetic: 0.07 us -> 1.24 us  [gathered_body(): (jnp.arange(frame_count, dtype=jnp.int32)[None, :] < counts[:, None]).ast...]
    gt x1, other arithmetic: 0.01 us -> 1.05 us  [gathered_body(): prev_wide = (prev_counts > 1)[:, None, None, None]]
  transfers between devices with their start and end apart: 3 -> 6, of which waited for: 0 -> 2; matrix products, arithmetic and copies ran while one was open for 11% -> 18% of each run, Pallas kernels for 0% -> 0%
where the time goes in v1:
time: 76.9 us; the launch traced here: 76.3 us
  local copies, waits for them, and re-layouts  16.6 us (22%)
  blocking collectives  16.6 us (22%)
  waiting for transfers between devices  12.9 us (17%)
  other arithmetic  10.2 us (13%)
  matrix products  10.1 us (13%)
  starting transfers between devices  9.36 us (12%)
    all_gather x1, blocking collectives, gathered_body(): inner_all = lax.all_gather(inner_input, 'rows', axis=2, tiled=True)  16.6 us
    ppermute x3, waiting for transfers between devices, series_fix(): inbox.append(ppermute(inbox[-1], axis_name=device_axis, perm=rack))  12.9 us
    dot_general x9, matrix products, convolve(): jnp.dot(columns.reshape(-1, 3 * channels), kernel, preferred_element_type...  7.16 us
    slice x1, local copies, waits for them, and re-layouts, convolve(): causal_weight[delta_time, delta_row].reshape(3 * channels, channels)  5.42 us
    unnamed x34, local copies, waits for them, and re-layouts  4.08 us
    ppermute x1, starting transfers between devices, gathered_body(): lax.ppermute(last_raw, 'tm', [(i, i + 2) for i in range(sections - 2)])  4 us
    slice x2, local copies, waits for them, and re-layouts, convolve(): window[:, :, :, delta_col:delta_col + column_count]  3.81 us
    ppermute x3, starting transfers between devices, series_fix(): inbox.append(ppermute(inbox[-1], axis_name=device_axis, perm=rack))  2.18 us
  transfers between devices with their start and end apart: 6, of which 2 were waited for; matrix products, arithmetic and copies ran while one was open for 18% of the time, Pallas kernels for 0%

profile of v1, /device:TPU:0, one launch (start us, length us, event | category | flops | bytes accessed | tf_op | source)
XLA Modules:
  0.0 76.3 jit_solution(4437852251152108982)
XLA Ops:
  0.0 16.6 %all_gather.3 = bf16[2,2,4,32,384]{4,3,2,1,0:T(8,128)(2,1)S(1)} all-gather(bf16[2,2,1,32,384]{4,3,2,1,0:T(8,128)(2,1)} %param.12), channel_id=1, replica_groups=mesh['clips'=2,'tm'=4,'rows'=4] {'rows'}, dimensions={2}, use_global_device_ids=true | all-gather | bytes 491520 | tf_op jit(solution)/shard_map/all_gather | solution.py:208
  17.4 1.3 %collective-permute-start.4 = (bf16[2,2,4,32,384]{4,3,2,0,1:T(8,128)(2,1)}, bf16[2,2,4,32,384]{4,3,2,0,1:T(8,128)(2,1)S(1)}, u32[]{:S(2)}, u32[]{:S(2)}) collective-permute-start(bf16[2,2,4,32,384]{4,3,2,0,1:T(8,128)(2,1)} %copy.75), channel_id=1, source_target_pairs={{0,4},{4,8},{8,12},{1,5},{5,9},{9,13},{2,6},{6,10},{10,14},{3,7},{... | collective-permute-start | bytes 1179656 | tf_op jit(solution)/shard_map/ppermute | solution.py:226
  19.4 0.8 %fusion.46 = bf16[2,4,32,384]{3,2,1,0:T(8,128)(2,1)} fusion(pred[2]{0:T(512)(128)(4,1)S(1)} %broadcast_compare_fusion, bf16[2,2,4,32,384]{4,3,2,1,0:T(8,128)(2,1)S(1)} %all_gather.3), kind=kLoop, calls=%fused_computation.108 | loop fusion | flops 98304 | bytes 589826 | tf_op jit(solution)/shard_map/jit(_where)/select_n | solution.py:225
  20.2 4.0 %collective-permute-start.5 = (bf16[2,4,32,384]{3,2,1,0:T(8,128)(2,1)}, bf16[2,4,32,384]{3,2,1,0:T(8,128)(2,1)S(1)}, u32[]{:S(2)}, u32[]{:S(2)}) collective-permute-start(bf16[2,4,32,384]{3,2,1,0:T(8,128)(2,1)} %fusion.46), channel_id=1, source_target_pairs={{0,8},{4,12},{1,9},{5,13},{2,10},{6,14},{3,11},{7,15},{16,24},{20,... | collective-permute-start | bytes 589832 | tf_op jit(solution)/shard_map/ppermute | solution.py:228
  24.2 1.9 %collective-permute-start.3 = (s32[2]{0:T(128)}, s32[2]{0:T(128)}, u32[]{:S(2)}, u32[]{:S(2)}) collective-permute-start(s32[2]{0:T(128)} %bitcast.12), channel_id=1, source_target_pairs={{0,4},{4,8},{8,12},{1,5},{5,9},{9,13},{2,6},{6,10},{10,14},{3,7},{... | collective-permute-start | bytes 32 | tf_op jit(solution)/shard_map/ppermute | solution.py:227
  26.1 2.2 %collective-permute-start = (bf16[2,2,1,32,384]{4,3,1,0,2:T(8,128)(2,1)S(1)}, bf16[2,2,1,32,384]{4,3,1,0,2:T(8,128)(2,1)}, u32[]{:S(2)}, u32[]{:S(2)}) collective-permute-start(bf16[2,2,1,32,384]{4,3,1,0,2:T(8,128)(2,1)S(1)} %bitcast.130), channel_id=1, source_target_pairs={{0,1},{1,2},{2,3},{3,0},{4,5},{5,6},{6,7},{7,4},{8,9},{9,10},{10,1... | collective-permute-start | bytes 294920 | tf_op jit(solution)/shard_map/ppermute | solution.py:215
  28.4 1.2 %compare_convert_fusion = f32[2,2]{1,0:T(2,128)} fusion(s32[2]{0:T(128)} %bitcast.12), kind=kLoop, calls=%fused_computation.129 | loop fusion | flops 8 | bytes 24 | tf_op jit(solution)/shard_map/convert_element_type | solution.py:280
  29.7 5.4 %fusion.61 = (bf16[1,1,3,384,384]{4,3,2,1,0:T(8,128)(2,1)}, bf16[1,1,3,384,384]{4,3,2,1,0:T(8,128)(2,1)S(1)}, bf16[1,1,3,384,384]{4,3,2,1,0:T(8,128)(2,1)}, bf16...) fusion(bf16[3,3,3,384,384]{4,3,2,1,0:T(8,128)(2,1)} %param.15), kind=kLoop, calls=%fused_computation.138 | loop fusion | bytes 15925248 | tf_op jit(solution)/shard_map/slice | solution.py:114
  36.1 1.1 %broadcast_compare_fusion.1 = pred[2]{0:T(512)(128)(4,1)} fusion(s32[2]{0:T(128)} %collective-permute-done.3), kind=kLoop, calls=%fused_computation.136 | loop fusion | flops 2 | bytes 10 | tf_op jit(solution)/shard_map/gt | solution.py:232
  37.3 6.5 %collective-permute-done.1 = bf16[2,2,1,32,384]{4,3,1,0,2:T(8,128)(2,1)S(1)} collective-permute-done((bf16[2,2,1,32,384]{4,3,1,0,2:T(8,128)(2,1)}, bf16[2,2,1,32,384]{4,3,1,0,2:T(8,128)(2,1)S(1)}, u32[]{:S(2)}, u32[]{:S(2)}) %collective-permute-start.1) | collective-permute-done | bytes 98336 | tf_op jit(solution)/shard_map/ppermute | solution.py:215
  43.8 6.4 %collective-permute-done.2 = bf16[2,2,1,32,384]{4,3,1,0,2:T(8,128)(2,1)S(1)} collective-permute-done((bf16[2,2,1,32,384]{4,3,1,0,2:T(8,128)(2,1)S(1)}, bf16[2,2,1,32,384]{4,3,1,0,2:T(8,128)(2,1)S(1)}, u32[]{:S(2)}, u32[]{:S(2)}) %collective-permute-start.2) | collective-permute-done | bytes 98336 | tf_op jit(solution)/shard_map/ppermute | solution.py:215
  50.2 1.7 %maximum_bitcast_fusion = bf16[4,2,2,32,384]{4,3,2,1,0:T(8,128)(2,1)} fusion(bf16[1,2,2,1,32,384]{5,4,2,1,0,3:T(8,128)(2,1)S(1)} %bitcast.133, bf16[1,2,2,1,32,384]{5,4,2,1,0,3:T(8,128)(2,1)S(1)} %bitcast.132, bf16[1,2,2,1,32,384]{5,4,2,1,0,3:T(8,128)(2,1)} %bitcast.3, bf16[1,2,2,1,32,384]{5,4,2,1,0,3:T(8,128)(2,1)S(1)} %bitcast.131), kind=kLoop, calls=%fused_computation.97 | loop fusion | flops 589824 | bytes 786432 | tf_op jit(solution)/shard_map/stack | solution.py:217
  51.9 1.7 %gather_fusion = bf16[4,2,2,32,384]{4,3,2,1,0:T(8,128)(2,1)S(1)} fusion(bf16[4,2,2,32,384]{4,3,2,1,0:T(8,128)(2,1)} %maximum_bitcast_fusion, s32[1024]{0:T(1024)} %pad_clamp_fusion), kind=kCustom, calls=%fused_computation | custom fusion | bytes 786448 | tf_op jit(solution)/shard_map/gather | solution.py:218
  54.8 3.5 %pad_slice_fusion.1 = (bf16[2,2,4,32,384]{4,3,2,1,0:T(8,128)(2,1)S(1)}, bf16[2,2,4,32,384]{4,3,2,1,0:T(8,128)(2,1)S(1)}, bf16[2,2,4,32,384]{4,3,2,1,0:T(8,128)(2...) fusion(bf16[2,4,6,32,384]{4,3,2,1,0:T(8,128)(2,1)S(1)} %fusion.6), kind=kLoop, calls=%fused_computation.38 | loop fusion | bytes 9437184 | tf_op jit(solution)/shard_map/slice | solution.py:111
  58.9 0.9 %copy-done.8 = bf16[1,1,3,384,384]{4,3,2,1,0:T(8,128)(2,1)S(1)} copy-done((bf16[1,1,3,384,384]{4,3,2,1,0:T(8,128)(2,1)S(1)}, bf16[1,1,3,384,384]{4,3,2,1,0:T(8,128)(2,1)}, u32[]{:S(2)}) %copy-start.8) | copy-done | bytes 884760
  61.8 0.8 %convolution_add_fusion.8 = f32[512,384]{1,0:T(8,128)S(1)} fusion(f32[512,384]{1,0:T(8,128)S(1)} %fusion.64, bf16[512,1152]{1,0:T(8,128)(2,1)S(1)} %bitcast.109, bf16[1152,384]{1,0:T(8,128)(2,1)S(1)} %bitcast.121), kind=kOutput, calls=%fused_computation.16 | convolution fusion | flops 453181440 | bytes 3637248 | tf_op jit(solution)/shard_map/dot_general | solution.py:115
  63.0 0.8 %convolution_add_fusion.7 = f32[512,384]{1,0:T(8,128)S(1)} fusion(f32[512,384]{1,0:T(8,128)S(1)} %convolution_add_fusion.8, bf16[512,1152]{1,0:T(8,128)(2,1)S(1)} %bitcast.110, bf16[1152,384]{1,0:T(8,128)(2,1)S(1)} %bitcast.120), kind=kOutput, calls=%fused_computation.15 | convolution fusion | flops 453181440 | bytes 3637248 | tf_op jit(solution)/shard_map/dot_general | solution.py:115
  64.0 0.9 %copy-done.3 = bf16[1,1,3,384,384]{4,3,2,1,0:T(8,128)(2,1)S(1)} copy-done((bf16[1,1,3,384,384]{4,3,2,1,0:T(8,128)(2,1)S(1)}, bf16[1,1,3,384,384]{4,3,2,1,0:T(8,128)(2,1)}, u32[]{:S(2)}) %copy-start.3) | copy-done | bytes 884760
  66.1 0.8 %convolution_add_fusion.5 = f32[512,384]{1,0:T(8,128)S(1)} fusion(f32[512,384]{1,0:T(8,128)S(1)} %convolution_add_fusion.6, bf16[512,1152]{1,0:T(8,128)(2,1)S(1)} %bitcast.108, bf16[1152,384]{1,0:T(8,128)(2,1)S(1)} %bitcast.118), kind=kOutput, calls=%fused_computation.13 | convolution fusion | flops 453181440 | bytes 3637248 | tf_op jit(solution)/shard_map/dot_general | solution.py:115
  68.3 0.8 %convolution_add_fusion.3 = f32[512,384]{1,0:T(8,128)S(1)} fusion(f32[512,384]{1,0:T(8,128)S(1)} %convolution_add_fusion.4, bf16[512,1152]{1,0:T(8,128)(2,1)S(1)} %bitcast.113, bf16[1152,384]{1,0:T(8,128)(2,1)S(1)} %bitcast.116), kind=kOutput, calls=%fused_computation.11 | convolution fusion | flops 453181440 | bytes 3637248 | tf_op jit(solution)/shard_map/dot_general | solution.py:115
  69.2 0.8 %convolution_add_fusion.2 = f32[512,384]{1,0:T(8,128)S(1)} fusion(f32[512,384]{1,0:T(8,128)S(1)} %convolution_add_fusion.3, bf16[512,1152]{1,0:T(8,128)(2,1)S(1)} %bitcast.107, bf16[1152,384]{1,0:T(8,128)(2,1)S(1)} %bitcast.115), kind=kOutput, calls=%fused_computation.10 | convolution fusion | flops 453181440 | bytes 3637248 | tf_op jit(solution)/shard_map/dot_general | solution.py:115
  70.3 0.8 %fusion.25 = (bf16[512,384]{1,0:T(8,128)(2,1)S(1)}, f32[512,384]{1,0:T(8,128)S(1)}) fusion(f32[2,2,4,1,32,384]{5,4,2,1,0,3:T(8,128)S(1)} %copy.88, f32[384]{0:T(512)S(1)} %copy-done.13, f32[512,384]{1,0:T(8,128)S(1)} %convolution_add_fusion.2, bf16[512,1152]{1,0:T(8,128)(2,1)S(1)} %bitcast.114, bf16[1152,384]{1,0:T(8,128)(2,1)S(1)} %bitcast.122), kind=kOutput, calls=%fused_computation.76 | convolution fusion | flops 453771264 | bytes 4818432 | tf_op jit(solution)/shard_map/dot_general | solution.py:115
  72.5 1.3 %convolution_add_fusion = f32[512,768]{1,0:T(8,128)S(1)} fusion(f32[768]{0:T(1024)S(1)} %slice.227, bf16[384,1152]{1,0:T(8,128)(2,1)S(1)} %copy-done.7, bf16[512,384]{1,0:T(8,128)(2,1)S(1)} %get-tuple-element.43, f32[384]{0:T(512)S(1)} %copy-done.11, f32[512]{0:T(512)} %rsqrt.40), kind=kOutput, calls=%fused_computation.5 | convolution fusion | flops 303169536 | bytes 2564096 | tf_op jit(solution)/shard_map/dot_general | solution.py:250
  73.9 0.9 %convolution_multiply_fusion = f32[4,32,128]{2,1,0:T(8,128)S(1)} fusion(f32[4,32,384]{2,1,0:T(8,128)S(1)} %bitcast.126, f32[4,128,768]{2,1,0:T(8,128)S(1)} %bitcast.105), kind=kOutput, calls=%fused_computation.36 | convolution fusion | flops 75513856 | bytes 1048576 | tf_op jit(solution)/shard_map/nqc,nkc->nqk/dot_general | solution.py:265
  (79 shorter events, 12.7 us)
Async XLA Ops:
  0.0 75.3 %copy-start = (bf16[384,384]{1,0:T(8,128)(2,1)S(1)}, bf16[384,384]{1,0:T(8,128)(2,1)}, u32[]{:S(2)}) copy-start(bf16[384,384]{1,0:T(8,128)(2,1)} %param.20) | copy-start | bytes 884740
  0.0 26.1 %copy-start.9 = (bf16[2,2,1,32,384]{4,3,2,1,0:T(8,128)(2,1)S(1)}, bf16[2,2,1,32,384]{4,3,2,1,0:T(8,128)(2,1)}, u32[]{:S(2)}) copy-start(bf16[2,2,1,32,384]{4,3,2,1,0:T(8,128)(2,1)} %param.11) | copy-start | bytes 294916
  0.0 28.4 %copy-start.12 = (f32[1152]{0:T(1024)S(1)}, f32[1152]{0:T(1024)}, u32[]{:S(2)}) copy-start(f32[1152]{0:T(1024)} %param.19) | copy-start | bytes 13828
  17.4 36.4 %collective-permute-start.4 = (bf16[2,2,4,32,384]{4,3,2,0,1:T(8,128)(2,1)}, bf16[2,2,4,32,384]{4,3,2,0,1:T(8,128)(2,1)S(1)}, u32[]{:S(2)}, u32[]{:S(2)}) collective-permute-start(bf16[2,2,4,32,384]{4,3,2,0,1:T(8,128)(2,1)} %copy.75), channel_id=1, source_target_pairs={{0,4},{4,8},{8,12},{1,5},{5,9},{9,13},{2,6},{6,10},{10,14},{3,7},{... | collective-permute-start | bytes 1179656 | tf_op jit(solution)/shard_map/ppermute | solution.py:226
  20.2 17.0 %collective-permute-start.5 = (bf16[2,4,32,384]{3,2,1,0:T(8,128)(2,1)}, bf16[2,4,32,384]{3,2,1,0:T(8,128)(2,1)S(1)}, u32[]{:S(2)}, u32[]{:S(2)}) collective-permute-start(bf16[2,4,32,384]{3,2,1,0:T(8,128)(2,1)} %fusion.46), channel_id=1, source_target_pairs={{0,8},{4,12},{1,9},{5,13},{2,10},{6,14},{3,11},{7,15},{16,24},{20,... | collective-permute-start | bytes 589832 | tf_op jit(solution)/shard_map/ppermute | solution.py:228
  24.2 11.9 %collective-permute-start.3 = (s32[2]{0:T(128)}, s32[2]{0:T(128)}, u32[]{:S(2)}, u32[]{:S(2)}) collective-permute-start(s32[2]{0:T(128)} %bitcast.12), channel_id=1, source_target_pairs={{0,4},{4,8},{8,12},{1,5},{5,9},{9,13},{2,6},{6,10},{10,14},{3,7},{... | collective-permute-start | bytes 32 | tf_op jit(solution)/shard_map/ppermute | solution.py:227
  26.1 11.1 %collective-permute-start = (bf16[2,2,1,32,384]{4,3,1,0,2:T(8,128)(2,1)S(1)}, bf16[2,2,1,32,384]{4,3,1,0,2:T(8,128)(2,1)}, u32[]{:S(2)}, u32[]{:S(2)}) collective-permute-start(bf16[2,2,1,32,384]{4,3,1,0,2:T(8,128)(2,1)S(1)} %bitcast.130), channel_id=1, source_target_pairs={{0,1},{1,2},{2,3},{3,0},{4,5},{5,6},{6,7},{7,4},{8,9},{9,10},{10,1... | collective-permute-start | bytes 294920 | tf_op jit(solution)/shard_map/ppermute | solution.py:215
  29.7 6.1 %copy-start.10 = (f32[384]{0:T(512)S(1)}, f32[384]{0:T(512)}, u32[]{:S(2)}) copy-start(f32[384]{0:T(512)} %param.14) | copy-start | bytes 4612
  37.2 6.6 %collective-permute-start.1 = (bf16[2,2,1,32,384]{4,3,1,0,2:T(8,128)(2,1)}, bf16[2,2,1,32,384]{4,3,1,0,2:T(8,128)(2,1)S(1)}, u32[]{:S(2)}, u32[]{:S(2)}) collective-permute-start(bf16[2,2,1,32,384]{4,3,1,0,2:T(8,128)(2,1)} %collective-permute-done), channel_id=1, source_target_pairs={{0,1},{1,2},{2,3},{3,0},{4,5},{5,6},{6,7},{7,4},{8,9},{9,10},{10,1... | collective-permute-start | bytes 294920 | tf_op jit(solution)/shard_map/ppermute | solution.py:215
  43.8 6.4 %collective-permute-start.2 = (bf16[2,2,1,32,384]{4,3,1,0,2:T(8,128)(2,1)S(1)}, bf16[2,2,1,32,384]{4,3,1,0,2:T(8,128)(2,1)S(1)}, u32[]{:S(2)}, u32[]{:S(2)}) collective-permute-start(bf16[2,2,1,32,384]{4,3,1,0,2:T(8,128)(2,1)S(1)} %collective-permute-done.1), channel_id=1, source_target_pairs={{0,1},{1,2},{2,3},{3,0},{4,5},{5,6},{6,7},{7,4},{8,9},{9,10},{10,1... | collective-permute-start | bytes 294920 | tf_op jit(solution)/shard_map/ppermute | solution.py:215
  53.7 0.6 copy-start.15
  58.7 1.2 %copy-start.8 = (bf16[1,1,3,384,384]{4,3,2,1,0:T(8,128)(2,1)S(1)}, bf16[1,1,3,384,384]{4,3,2,1,0:T(8,128)(2,1)}, u32[]{:S(2)}) copy-start(bf16[1,1,3,384,384]{4,3,2,1,0:T(8,128)(2,1)} %get-tuple-element.14) | copy-start | bytes 2654212
  60.6 1.2 %copy-start.5 = (bf16[1,1,3,384,384]{4,3,2,1,0:T(8,128)(2,1)S(1)}, bf16[1,1,3,384,384]{4,3,2,1,0:T(8,128)(2,1)}, u32[]{:S(2)}) copy-start(bf16[1,1,3,384,384]{4,3,2,1,0:T(8,128)(2,1)} %get-tuple-element.13) | copy-start | bytes 2654212
  61.8 1.2 %copy-start.4 = (bf16[1,1,3,384,384]{4,3,2,1,0:T(8,128)(2,1)S(1)}, bf16[1,1,3,384,384]{4,3,2,1,0:T(8,128)(2,1)}, u32[]{:S(2)}) copy-start(bf16[1,1,3,384,384]{4,3,2,1,0:T(8,128)(2,1)} %get-tuple-element.12) | copy-start | bytes 2654212
  63.8 1.2 %copy-start.3 = (bf16[1,1,3,384,384]{4,3,2,1,0:T(8,128)(2,1)S(1)}, bf16[1,1,3,384,384]{4,3,2,1,0:T(8,128)(2,1)}, u32[]{:S(2)}) copy-start(bf16[1,1,3,384,384]{4,3,2,1,0:T(8,128)(2,1)} %get-tuple-element.11) | copy-start | bytes 2654212
  64.9 1.2 %copy-start.2 = (bf16[1,1,3,384,384]{4,3,2,1,0:T(8,128)(2,1)S(1)}, bf16[1,1,3,384,384]{4,3,2,1,0:T(8,128)(2,1)}, u32[]{:S(2)}) copy-start(bf16[1,1,3,384,384]{4,3,2,1,0:T(8,128)(2,1)} %get-tuple-element.10) | copy-start | bytes 2654212
  66.1 1.2 %copy-start.1 = (bf16[1,1,3,384,384]{4,3,2,1,0:T(8,128)(2,1)S(1)}, bf16[1,1,3,384,384]{4,3,2,1,0:T(8,128)(2,1)}, u32[]{:S(2)}) copy-start(bf16[1,1,3,384,384]{4,3,2,1,0:T(8,128)(2,1)} %get-tuple-element.9) | copy-start | bytes 2654212
  69.1 1.2 %copy-start.6 = (bf16[1,1,3,384,384]{4,3,2,1,0:T(8,128)(2,1)S(1)}, bf16[1,1,3,384,384]{4,3,2,1,0:T(8,128)(2,1)}, u32[]{:S(2)}) copy-start(bf16[1,1,3,384,384]{4,3,2,1,0:T(8,128)(2,1)} %get-tuple-element.7) | copy-start | bytes 2654212
  69.1 1.2 %copy-start.13 = (f32[384]{0:T(512)S(1)}, f32[384]{0:T(512)}, u32[]{:S(2)}) copy-start(f32[384]{0:T(512)} %param.16) | copy-start | bytes 4612
  71.1 1.0 %copy-start.11 = (f32[384]{0:T(512)S(1)}, f32[384]{0:T(512)}, u32[]{:S(2)}) copy-start(f32[384]{0:T(512)} %param.17) | copy-start | bytes 4612
  71.1 1.2 %copy-start.7 = (bf16[384,1152]{1,0:T(8,128)(2,1)S(1)}, bf16[384,1152]{1,0:T(8,128)(2,1)}, u32[]{:S(2)}) copy-start(bf16[384,1152]{1,0:T(8,128)(2,1)} %param.18) | copy-start | bytes 2654212
  71.1 1.2 %slice-start = ((f32[1152]{0:T(1024)}), f32[384]{0:T(512)S(1)}, s32[]{:S(2)}) async-start(f32[1152]{0:T(1024)} %param.19), calls=%async_computation | async-start | bytes 4096 | tf_op jit(solution)/shard_map/slice | solution.py:263
  73.8 1.5 %copy-start.14 = (f32[384]{0:T(512)S(1)}, f32[384]{0:T(512)}, u32[]{:S(2)}) copy-start(f32[384]{0:T(512)} %param.21) | copy-start | bytes 4612
  73.9 1.7 %copy-start.16 = (f32[2,2]{1,0:T(2,128)S(1)}, f32[2,2]{1,0:T(2,128)}, u32[]{:S(2)}) copy-start(f32[2,2]{1,0:T(2,128)} %compare_convert_fusion) | copy-start | bytes 52
